TPU v7x, 32 devices: a whole 2x2x4 slice. The times are simulated.
32 devices in a mesh: real: 2 (over x), los: 8 (over z, y), sky: 2 (over core).
Axes of the slice: x: 2, y: 2, z: 4, core: 2. Of those that a mesh axis runs over, the one named last changes fastest.
Arguments:
- density: float32 [16, 2048, 2048], P(('real', 'los'), 'sky'), parts along dimension 0, may hold values from -6 to 8
- lens_weight: float32 [16], P(('real', 'los')), parts along dimension 0, may hold values from 0.05 to 0.4
- plane_count: int32 [16], P(('real', 'los')), parts along dimension 0, may hold values from 0 to 1
- ray_state: float32 [16, 12, 32, 2048], P(('real', 'los'), None, 'sky'), parts along dimension 0, may hold values from -6 to 6
Outputs:
- ray_out: float32 [16, 12, 32, 2048], P(('real', 'los'), None, 'sky'), parts along dimension 0
There are 2 independent parts, one for each index of `real`. A program takes and returns all parts, laid end to end along the dimension named above; each array names one. Nothing has to cross between parts.
All inputs are finite; a program needn't handle non-finite values.
Results may differ from a plain program's by a relative error of at most 0.00012.
Values sent between devices are 32-bit elements; how exact they have to be, the bound alone decides.
No kernel may reach another device: no remote copies, remote signals or barrier semaphores. Data moves between devices by JAX's collectives and lax.ppermute only.
A program may use at most 128 MiB of HBM per device.

v0:
```python
import math
import jax
import jax.numpy as jnp
from jax import lax
from jax.sharding import PartitionSpec as P

HOPS = 4
two_pi = 2.0 * math.pi
highest = lax.Precision.HIGH
first_radix = 16


def shifted(block, axis, distance):
    devices = range(lax.axis_size(axis))
    route = [((i - distance) % len(devices), i) for i in devices]
    return lax.ppermute(block, axis, route)


def lens_step(ray_tile, fields):
    disp_x = ray_tile[..., 0, :, :]
    disp_y = ray_tile[..., 1, :, :]
    tilt_x = ray_tile[..., 2, :, :]
    tilt_y = ray_tile[..., 3, :, :]
    jac_xx = ray_tile[..., 4, :, :]
    jac_xy = ray_tile[..., 5, :, :]
    jac_yx = ray_tile[..., 6, :, :]
    jac_yy = ray_tile[..., 7, :, :]
    rate_xx = ray_tile[..., 8, :, :]
    rate_xy = ray_tile[..., 9, :, :]
    rate_yx = ray_tile[..., 10, :, :]
    rate_yy = ray_tile[..., 11, :, :]
    bend_x = fields[..., 0, :, :]
    bend_y = fields[..., 1, :, :]
    hess_xx = fields[..., 2, :, :]
    hess_yy = fields[..., 3, :, :]
    hess_xy = fields[..., 4, :, :]
    push_x = bend_x + hess_xx * disp_x + hess_xy * disp_y
    push_y = bend_y + hess_xy * disp_x + hess_yy * disp_y
    new_tilt_x = tilt_x - push_x
    new_tilt_y = tilt_y - push_y
    new_disp_x = disp_x + new_tilt_x
    new_disp_y = disp_y + new_tilt_y
    new_rate_xx = rate_xx - (hess_xx * jac_xx + hess_xy * jac_yx)
    new_rate_xy = rate_xy - (hess_xx * jac_xy + hess_xy * jac_yy)
    new_rate_yx = rate_yx - (hess_xy * jac_xx + hess_yy * jac_yx)
    new_rate_yy = rate_yy - (hess_xy * jac_xy + hess_yy * jac_yy)
    new_jac_xx = jac_xx + new_rate_xx
    new_jac_xy = jac_xy + new_rate_xy
    new_jac_yx = jac_yx + new_rate_yx
    new_jac_yy = jac_yy + new_rate_yy
    return jnp.stack(
        [
            new_disp_x,
            new_disp_y,
            new_tilt_x,
            new_tilt_y,
            new_jac_xx,
            new_jac_xy,
            new_jac_yx,
            new_jac_yy,
            new_rate_xx,
            new_rate_xy,
            new_rate_yx,
            new_rate_yy,
        ],
        axis=-3,
    )


def phase_table(left_idx, right_idx, modulus, orient):
    product = left_idx[:, None] * right_idx[None, :] % modulus
    angle = orient * two_pi / modulus * product.astype(jnp.float32)
    return (jnp.cos(angle), jnp.sin(angle))


def block_table(left_idx, right_idx, modulus, orient):
    t_re, t_im = phase_table(left_idx, right_idx, modulus, orient)
    top = jnp.concatenate([t_re, t_im], axis=1)
    bottom = jnp.concatenate([-t_im, t_re], axis=1)
    return jnp.concatenate([top, bottom], axis=0)


def mixed(form, left_op, right_op):
    return jnp.einsum(
        form, left_op, right_op, precision=highest, preferred_element_type=jnp.float32
    )


def complex_product(form, real_in, imag_in, table_re, table_im):
    if imag_in is None:
        return (mixed(form, real_in, table_re), mixed(form, real_in, table_im))
    out_re = mixed(form, real_in, table_re) - mixed(form, imag_in, table_im)
    out_im = mixed(form, real_in, table_im) + mixed(form, imag_in, table_re)
    return (out_re, out_im)


def first_factor_of(length):
    factor_one = 1
    while factor_one * factor_one < length and length % (factor_one * 2) == 0:
        factor_one = factor_one * 2
    return factor_one


def rows_forward(cells):
    row_count, length = cells.shape
    second = length // first_radix
    half = second // 2
    shaped = cells.reshape(row_count, first_radix, second)
    v_idx = jnp.arange(first_radix, dtype=jnp.int32)
    u_idx = jnp.arange(second, dtype=jnp.int32)
    m_idx = jnp.arange(half, dtype=jnp.int32)
    section_re, section_im = phase_table(v_idx, v_idx, first_radix, -1.0)
    part_re = mixed("rvu,vk->rku", shaped, section_re)
    part_im = mixed("rvu,vk->rku", shaped, section_im)
    twist_re, twist_im = phase_table(v_idx, u_idx, length, -1.0)
    turned_re = part_re * twist_re - part_im * twist_im
    turned_im = part_re * twist_im + part_im * twist_re
    final = block_table(u_idx, m_idx, second, -1.0)
    return mixed("rkj,jn->rkn", turned_re, final[:second]) + mixed(
        "rkj,jn->rkn", turned_im, final[second:]
    )


def columns_forward(spread_re, spread_im):
    length, col_count = spread_re.shape
    factor_one = first_factor_of(length)
    second = length // factor_one
    first_idx = jnp.arange(factor_one, dtype=jnp.int32)
    second_idx = jnp.arange(second, dtype=jnp.int32)
    section = block_table(first_idx, first_idx, factor_one, -1.0)
    part = mixed(
        "jn,jbc->nbc", section[:factor_one], spread_re.reshape(factor_one, second, col_count)
    ) + mixed("jn,jbc->nbc", section[factor_one:], spread_im.reshape(factor_one, second, col_count))
    part = part.reshape(2, factor_one, second, col_count)
    twist_re, twist_im = phase_table(first_idx, second_idx, length, -1.0)
    twist_re = twist_re[:, :, None]
    twist_im = twist_im[:, :, None]
    turned_re = part[0] * twist_re - part[1] * twist_im
    turned_im = part[0] * twist_im + part[1] * twist_re
    turned = jnp.stack([turned_re, turned_im], axis=1).reshape(factor_one, 2 * second, col_count)
    final = block_table(second_idx, second_idx, second, -1.0)
    done = mixed("kjc,jn->knc", turned, final)
    return done.reshape(factor_one, 2, second, col_count)


def rows_inverse(spec_re, spec_im, length, m_count):
    row_count = spec_re.shape[0]
    second = length // first_radix
    shaped_re = spec_re.reshape(row_count, first_radix, m_count)
    shaped_im = spec_im.reshape(row_count, first_radix, m_count)
    k_idx = jnp.arange(first_radix, dtype=jnp.int32)
    u_idx = jnp.arange(second, dtype=jnp.int32)
    m_idx = jnp.arange(m_count, dtype=jnp.int32)
    section_re, section_im = phase_table(m_idx, u_idx, second, 1.0)
    part_re, part_im = complex_product("rkm,mu->rku", shaped_re, shaped_im, section_re, section_im)
    twist_re, twist_im = phase_table(k_idx, u_idx, length, 1.0)
    turned_re = part_re * twist_re - part_im * twist_im
    turned_im = part_re * twist_im + part_im * twist_re
    final_re, final_im = phase_table(k_idx, k_idx, first_radix, 1.0)
    done_re, done_im = complex_product("rku,kv->rvu", turned_re, turned_im, final_re, final_im)
    return (done_re.reshape(row_count, length), done_im.reshape(row_count, length))


def wavenumbers(indices, length):
    signed = jnp.where(indices < length // 2, indices, indices - length)
    return (two_pi / length * signed.astype(jnp.float32), indices != length // 2)


def folded_spectra(spectrum, col_idx, ray_all):
    k_count, _, m_count, col_count = spectrum.shape
    length = k_count * m_count
    norm_factor = float(length * length)
    wave_col, retain_col = wavenumbers(col_idx, length)
    weight = jnp.where(col_idx == 0, 1.0, 2.0).astype(jnp.float32)
    row_idx = (
        jnp.arange(k_count, dtype=jnp.int32)[:, None]
        + k_count * jnp.arange(m_count, dtype=jnp.int32)[None, :]
    )
    wave_row, retain_row = wavenumbers(row_idx, length)
    wave_row = wave_row[:, None, :, None]
    retain_row = retain_row[:, None, :, None]
    squared = wave_col * wave_col + wave_row * wave_row
    retain = retain_row & retain_col & (squared > 0.0)
    safe_sq = jnp.where(retain, squared, 1.0)
    kernel = jnp.where(retain, -2.0 / (safe_sq * norm_factor), 0.0) * weight
    phi = kernel * spectrum
    terms = jnp.stack([phi, wave_row * phi, wave_row * wave_row * phi])
    terms = terms.reshape(3, k_count // ray_all, ray_all, 2, m_count, col_count)
    return jnp.transpose(jnp.sum(terms, axis=(1, 4)), (0, 2, 1, 3))


def per_device(density, lens_weight, plane_count, ray_state):
    sky_count = lax.axis_size("sky")
    sky_index = lax.axis_index("sky")
    ray_split = ray_state.shape[1] // 3
    ray_first = shifted(ray_state[:, :ray_split], "los", HOPS)
    ray_second = shifted(ray_state[:, ray_split:], "los", HOPS)
    plane_cells = density[0]
    length = plane_cells.shape[1]
    second = length // first_radix
    half = second // 2
    ray_dev = ray_state.shape[2]
    ray_all = ray_dev * sky_count
    strength = lens_weight[0] * plane_count[0].astype(jnp.float32)
    rows = rows_forward(plane_cells)
    ray_first, rows = lax.optimization_barrier((ray_first, rows))
    spread = lax.all_to_all(rows, "sky", split_axis=1, concat_axis=0, tiled=True)
    k_local = spread.shape[1]
    spread_re = spread[:, :, :half].reshape(length, k_local * half)
    spread_im = spread[:, :, half:].reshape(length, k_local * half)
    spectrum = columns_forward(spread_re, spread_im)
    ray_second, spectrum = lax.optimization_barrier((ray_second, spectrum))
    position = jnp.arange(k_local * half, dtype=jnp.int32)
    col_idx = sky_index * k_local + position // half + first_radix * (position % half)
    folds = folded_spectra(spectrum, col_idx, ray_all)
    q_idx = jnp.arange(ray_all, dtype=jnp.int32)
    back = block_table(q_idx, q_idx, ray_all, 1.0)
    at_rows = mixed("pjc,jn->pnc", folds.reshape(3, 2 * ray_all, k_local * half), back)
    at_rows = at_rows.reshape(3, 2, ray_all, k_local, half)
    returned = lax.all_to_all(at_rows, "sky", split_axis=2, concat_axis=3, tiled=True)
    k_all = returned.shape[3]
    dense = returned.reshape(3 * 2 * ray_dev, k_all * half) * strength
    arrived = jnp.stack(
        [shifted(dense, "los", HOPS - step_index) for step_index in range(HOPS)]
    ).reshape(HOPS, 3, 2, ray_dev, k_all, half)
    kx_idx = (
        jnp.arange(k_all, dtype=jnp.int32)[:, None]
        + first_radix * jnp.arange(half, dtype=jnp.int32)[None, :]
    )
    wave_col = wavenumbers(kx_idx, length)[0]
    f0_re, f0_im = (arrived[:, 0, 0], arrived[:, 0, 1])
    f1_re, f1_im = (arrived[:, 1, 0], arrived[:, 1, 1])
    f2_re, f2_im = (arrived[:, 2, 0], arrived[:, 2, 1])
    col_sq = wave_col * wave_col
    all_re = jnp.stack(
        [-wave_col * f0_im, -f1_im, -col_sq * f0_re, -f2_re, -wave_col * f1_re], axis=1
    )
    all_im = jnp.stack(
        [wave_col * f0_re, f1_re, -col_sq * f0_im, -f2_im, -wave_col * f1_im], axis=1
    )
    flat_re = all_re.reshape(HOPS * 5 * ray_dev, k_all * half)
    flat_im = all_im.reshape(HOPS * 5 * ray_dev, k_all * half)
    field_re, _ = rows_inverse(flat_re, flat_im, length, half)
    fields = field_re.reshape(HOPS, 5, ray_dev, length)
    ray_tile = jnp.concatenate([ray_first, ray_second], axis=1)
    for step_index in range(HOPS):
        ray_tile = lens_step(ray_tile, fields[step_index][None])
    return ray_tile


def solution(mesh):
    return jax.shard_map(
        per_device,
        mesh=mesh,
        in_specs=(
            P(("real", "los"), "sky", None),
            P(("real", "los")),
            P(("real", "los")),
            P(("real", "los"), None, "sky", None),
        ),
        out_specs=P(("real", "los"), None, "sky", None),
        check_vma=False,
    )
```

profile of v0, /device:TPU:0, one launch (start us, length us, event | category | flops | bytes accessed | tf_op | source)
XLA Modules:
  0.0 212.5 jit_solution(7195133602715866516)
XLA Ops:
  0.0 1.9 slice.160
  1.9 4.0 %collective-permute-start = (f32[1,4,16,2048]{3,2,1,0:T(8,128)}, f32[1,4,16,2048]{3,2,1,0:T(8,128)S(1)}, u32[]{:S(2)}, u32[]{:S(2)}) collective-permute-start(f32[1,4,16,2048]{3,2,1,0:T(8,128)} %slice.160), channel_id=1, source_target_pairs={{8,0},{10,2},{12,4},{14,6},{0,8},{2,10},{4,12},{6,14},{9,1},{11,3}... | collective-permute-start | bytes 1572872 | tf_op jit(solution)/shard_map/ppermute | solution.py:16
  5.9 2.3 %slice.163 = f32[1,8,16,2048]{3,2,1,0:T(8,128)} slice(f32[1,12,16,2048]{3,2,1,0:T(8,128)} %param.7), slice={[0:1], [4:12], [0:16], [0:2048]} | slice | bytes 2097152 | tf_op jit(solution)/shard_map/slice | solution.py:197
  8.3 0.3 fusion.109
  8.6 0.3 fusion.113
  8.8 0.1 fusion.128
  9.0 0.1 fusion.127
  9.7 5.4 %copy.96 = f32[128,8,16,128]{3,2,1,0:T(8,128)S(1)} copy(f32[128,8,16,128]{3,1,2,0:T(8,128)} %bitcast.162) | data formatting | bytes 16777216
  15.0 6.0 %fusion.143 = f32[16,1024,128]{2,0,1:T(8,128)} fusion(f32[1024,16,128]{2,1,0:T(8,128)S(1)} %bitcast.149), kind=kOutput, calls=%fused_computation.239 | convolution fusion | flops 201330176 | bytes 16777216 | tf_op jit(solution)/shard_map/rvu,vk->rku/dot_general | solution.py:84
  22.4 10.8 %subtract_bitcast_fusion = (f32[1024,16,128]{2,1,0:T(8,128)}, f32[1024,16,128]{2,1,0:T(8,128)}) fusion(f32[16,1024,128]{2,0,1:T(8,128)} %fusion.143, f32[16,128]{1,0:T(8,128)S(1)} %get-tuple-element.89, f32[16,128]{1,0:T(8,128)S(1)} %get-tuple-element.90, f32[1024,16,128]{2,1,0:T(8,128)S(1)} %bitcast.150), kind=kOutput, calls=%fused_computation.9 | convolution fusion | flops 213913088 | bytes 33570816 | tf_op jit(solution)/shard_map/rvu,vk->rku/dot_general | solution.py:84
  33.2 9.6 %fusion.2 = f32[1024,16,128]{2,0,1:T(8,128)S(1)} fusion(f32[1024,16,128]{2,1,0:T(8,128)} %get-tuple-element.58, f32[128,64]{1,0:T(8,128)S(1)} %get-tuple-element.92, f32[128,64]{1,0:T(8,128)S(1)} %fusion.113), kind=kOutput, calls=%fused_computation.4 | convolution fusion | flops 1610629120 | bytes 16842752 | tf_op jit(solution)/shard_map/rkj,jn->rkn/dot_general | solution.py:84
  42.9 5.6 %fusion.15 = f32[1024,16,128]{2,0,1:T(8,128)S(1)} fusion(f32[1024,16,128]{2,0,1:T(8,128)S(1)} %fusion.2, f32[1024,16,128]{2,1,0:T(8,128)S(1)} %bitcast.155, f32[128,64]{1,0:T(8,128)S(1)} %get-tuple-element.91, f32[128,64]{1,0:T(8,128)S(1)} %get-tuple-element.92), kind=kOutput, calls=%fused_computation.26 | convolution fusion | flops 1612726272 | bytes 25231360 | tf_op jit(solution)/shard_map/rkj,jn->rkn/dot_general | solution.py:84
  48.4 3.6 %fusion.9 = f32[64,32,512]{2,1,0:T(8,128)} fusion(f32[512]{0:T(512)S(1)} %get-tuple-element.100, f32[64,32]{1,0:T(8,128)S(1)} %get-tuple-element.87, f32[512]{0:T(512)S(1)} %get-tuple-element.99, pred[512]{0:T(512)(128)(4,1)S(1)} %broadcast_compare_fusion, pred[64,32]{1,0:T(8,128)(4,1)S(1)} %fusion.108), kind=kLoop, calls=%fused_computation.15 | loop fusion | flops 9437184 | bytes 4209152 | tf_op jit(solution)/shard_map/mul | solution.py:185
  52.0 0.6 collective-permute-done
  52.6 10.9 %all_to_all.27 = f32[1024,16,128]{2,0,1:T(8,128)S(1)} all-to-all(f32[1024,16,128]{2,0,1:T(8,128)S(1)} %fusion.15), channel_id=1, replica_groups=mesh['real'=2,'los'=8,'sky'=2] {'sky'}, dimensions={1} | all-to-all | bytes 16777216 | tf_op jit(solution)/shard_map/all_to_all | solution.py:207
  63.5 4.9 %copy.76 = f32[1024,2,8,128]{3,2,0,1:T(8,128)S(1)} copy(f32[1024,2,8,128]{3,0,2,1:T(8,128)S(1)} %bitcast.157) | data formatting | bytes 16777216 | tf_op jit(solution)/shard_map/all_to_all | solution.py:207
  68.4 7.2 %fusion.237 = (f32[2048,8,64]{2,1,0:T(8,128)}, f32[2048,8,64]{2,1,0:T(8,128)}) fusion(f32[2048,8,128]{2,1,0:T(8,128)S(1)} %bitcast.148), kind=kLoop, calls=%fused_computation.331 | loop fusion | bytes 16777216 | tf_op jit(solution)/shard_map/slice | solution.py:209
  75.5 7.5 %reshape_reshape.14 = f32[64,32,512]{2,1,0:T(8,128)} reshape(f32[2048,8,64]{2,1,0:T(8,128)} %get-tuple-element.62) | data formatting | bytes 8388608 | tf_op jit(solution)/shard_map/reshape;reshape | solution.py:133
  83.0 7.5 %reshape_reshape.13 = f32[64,32,512]{2,1,0:T(8,128)} reshape(f32[2048,8,64]{2,1,0:T(8,128)} %get-tuple-element.61) | data formatting | bytes 8388608 | tf_op jit(solution)/shard_map/reshape;reshape | solution.py:132
  90.5 9.4 %fusion.10 = f32[128,32,512]{2,0,1:T(8,128)S(1)} fusion(f32[64,32,512]{2,1,0:T(8,128)} %reshape_reshape.14, f32[64,64]{1,0:T(8,128)S(1)} %get-tuple-element.93, f32[64,64]{1,0:T(8,128)S(1)} %get-tuple-element.94), kind=kOutput, calls=%fused_computation.16 | convolution fusion | flops 805314560 | bytes 12615680 | tf_op jit(solution)/shard_map/jn,jbc->nbc/dot_general | solution.py:84
  100.0 5.9 %fusion.18 = f32[128,32,512]{2,0,1:T(8,128)S(1)} fusion(f32[128,32,512]{2,0,1:T(8,128)S(1)} %fusion.10, f32[64,32,512]{2,1,0:T(8,128)S(1)} %copy-done, f32[64,64]{1,0:T(8,128)S(1)} %fusion.127, f32[64,64]{1,0:T(8,128)S(1)} %get-tuple-element.93), kind=kOutput, calls=%fused_computation.27 | convolution fusion | flops 807411712 | bytes 21004288 | tf_op jit(solution)/shard_map/jn,jbc->nbc/dot_general | solution.py:84
  105.9 1.1 subtract_bitcast_fusion.1
  107.1 1.8 pad_maximum_fusion
  108.9 8.7 %fusion = f32[64,64,512]{2,0,1:T(8,128)S(1)} fusion(f32[64,64,512]{2,0,1:T(8,128)S(1)} %bitcast.152, f32[32,32]{0,1:T(8,128)S(1)} %get-tuple-element.98, f32[32,32]{0,1:T(8,128)S(1)} %fusion.164, f32[32,32]{0,1:T(8,128)S(1)} %get-tuple-element.97), kind=kOutput, calls=%fused_computation.2 | convolution fusion | flops 805318656 | bytes 16789504 | tf_op jit(solution)/shard_map/kjc,jn->knc/dot_general | solution.py:84
  117.6 4.0 %broadcast_multiply_fusion.1 = (f32[64,2,32,512]{3,2,1,0:T(8,128)}, f32[64,2,32,512]{3,2,1,0:T(8,128)S(1)}) fusion(f32[64,32]{1,0:T(8,128)S(1)} %get-tuple-element.88, f32[64,2,32,512]{3,2,1,0:T(8,128)S(1)} %bitcast.153, f32[64,32,512]{2,1,0:T(8,128)S(1)} %copy-done.1), kind=kLoop, calls=%fused_computation.21 | loop fusion | flops 4194304 | bytes 29368320 | tf_op jit(solution)/shard_map/mul | solution.py:187
  121.6 0.6 broadcast_multiply_fusion
  122.3 7.4 %maximum_reduce_fusion = f32[3,32,2,512]{3,2,1,0:T(2,128)S(1)} fusion(f32[1,2,32,2,32,512]{5,4,3,2,1,0:T(8,128)S(1)} %bitcast.151, f32[1,2,32,2,32,512]{5,4,3,2,1,0:T(8,128)} %bitcast.156, f32[1,2,32,2,32,512]{5,4,3,2,1,0:T(8,128)S(1)} %bitcast.147), kind=kLoop, calls=%fused_computation | loop fusion | flops 18776064 | bytes 25559040 | tf_op jit(solution)/shard_map/reduce_sum | solution.py:189
  129.7 0.4 convolution_bitcast_fusion
  130.1 0.2 reshape.929
  130.3 0.5 reshape.942
  130.8 4.0 %all_to_all.28 = f32[2,1,49152]{2,1,0:T(1,128)S(1)} all-to-all(f32[2,1,49152]{2,1,0:T(1,128)S(1)} %reshape.942), channel_id=1, replica_groups=mesh['real'=2,'los'=8,'sky'=2] {'sky'}, dimensions={0} | all-to-all | bytes 786432 | tf_op jit(solution)/shard_map/all_to_all | solution.py:220
  134.9 0.6 broadcast.706
  135.4 1.9 reduce
  137.3 0.5 reshape.943
  137.9 0.2 mul.1433
  138.2 2.4 %collective-permute-start.2 = (f32[96,1024]{1,0:T(8,128)S(1)}, f32[96,1024]{1,0:T(8,128)S(1)}, u32[]{:S(2)}, u32[]{:S(2)}) collective-permute-start(f32[96,1024]{1,0:T(8,128)S(1)} %mul.1433), channel_id=1, source_target_pairs={{8,0},{10,2},{12,4},{14,6},{0,8},{2,10},{4,12},{6,14},{9,1},{11,3}... | collective-permute-start | bytes 1179656 | tf_op jit(solution)/shard_map/ppermute | solution.py:16
  140.6 2.5 %collective-permute-start.3 = (f32[96,1024]{1,0:T(8,128)S(1)}, f32[96,1024]{1,0:T(8,128)S(1)}, u32[]{:S(2)}, u32[]{:S(2)}) collective-permute-start(f32[96,1024]{1,0:T(8,128)S(1)} %mul.1433), channel_id=1, source_target_pairs={{10,0},{12,2},{14,4},{0,6},{2,8},{4,10},{6,12},{8,14},{11,1},{13,3... | collective-permute-start | bytes 1179656 | tf_op jit(solution)/shard_map/ppermute | solution.py:16
  143.1 1.0 collective-permute-start.5
  144.1 0.6 multiply_sine_fusion.2
  144.8 0.6 fusion.140
  145.4 30.2 %collective-permute-done.2 = f32[96,1024]{1,0:T(8,128)S(1)} collective-permute-done((f32[96,1024]{1,0:T(8,128)S(1)}, f32[96,1024]{1,0:T(8,128)S(1)}, u32[]{:S(2)}, u32[]{:S(2)}) %collective-permute-start.2) | collective-permute-done | bytes 393248 | tf_op jit(solution)/shard_map/ppermute | solution.py:16
  175.6 0.2 stack.73
  175.8 17.9 %collective-permute-done.3 = f32[96,1024]{1,0:T(8,128)S(1)} collective-permute-done((f32[96,1024]{1,0:T(8,128)S(1)}, f32[96,1024]{1,0:T(8,128)S(1)}, u32[]{:S(2)}, u32[]{:S(2)}) %collective-permute-start.3) | collective-permute-done | bytes 393248 | tf_op jit(solution)/shard_map/ppermute | solution.py:16
  193.7 0.2 stack.74
  194.0 0.2 stack.75
  194.2 0.2 stack.76
  194.4 0.3 pad_maximum_fusion.1
  194.7 0.4 copy-done.11
  195.2 0.2 copy-done.10
  195.7 1.3 fusion.102
  197.0 1.3 fusion.98
  198.3 1.3 convolution_subtract_fusion
  199.7 1.4 convolution_add_fusion
  201.1 1.3 fusion.21
  202.4 1.3 subtract_bitcast_fusion.2
  203.8 0.2 fusion.238
  204.0 0.1 slice.175
  204.1 0.1 slice.181
  204.3 2.2 %add_subtract_fusion.6 = (f32[1,1,16,2048]{3,2,1,0:T(8,128)S(1)}, f32[1,1,16,2048]{3,2,1,0:T(8,128)S(1)}, f32[1,1,16,2048]{3,2,1,0:T(8,128)S(1)}, f32[1,1,16,204...) fusion(f32[1,5,16,2048]{3,2,1,0:T(8,128)S(1)} %slice.181, f32[1,8,16,2048]{3,2,1,0:T(8,128)} %copy-done.2, ...), kind=kLoop, calls=%fused_computation.99 | loop fusion | flops 917504 | bytes 2490368 | tf_op jit(solution)/shard_map/sub | solution.py:44
  206.5 1.9 fusion.55
  208.6 1.2 fusion.51
  210.0 0.1 add_subtract_fusion.4
  210.4 1.1 copy-done.12
  211.6 0.7 constant_dynamic-update-slice_fusion
  (67 shorter events, 1.8 us)
Async XLA Ops:
  1.9 50.7 %collective-permute-start = (f32[1,4,16,2048]{3,2,1,0:T(8,128)}, f32[1,4,16,2048]{3,2,1,0:T(8,128)S(1)}, u32[]{:S(2)}, u32[]{:S(2)}) collective-permute-start(f32[1,4,16,2048]{3,2,1,0:T(8,128)} %slice.160), channel_id=1, source_target_pairs={{8,0},{10,2},{12,4},{14,6},{0,8},{2,10},{4,12},{6,14},{9,1},{11,3}... | collective-permute-start | bytes 1572872 | tf_op jit(solution)/shard_map/ppermute | solution.py:16
  8.2 109.4 %collective-permute-start.1 = (f32[1,8,16,2048]{3,2,1,0:T(8,128)}, f32[1,8,16,2048]{3,2,1,0:T(8,128)S(1)}, u32[]{:S(2)}, u32[]{:S(2)}) collective-permute-start(f32[1,8,16,2048]{3,2,1,0:T(8,128)} %slice.163), channel_id=1, source_target_pairs={{8,0},{10,2},{12,4},{14,6},{0,8},{2,10},{4,12},{6,14},{9,1},{11,3}... | collective-permute-start | bytes 3145736 | tf_op jit(solution)/shard_map/ppermute | solution.py:16
  33.2 9.6 %slice-start = ((s8[8388608]{0:T(1024)(128)(4,1)}), s8[4194304]{0:T(1024)(128)(4,1)S(1)}, s32[]{:S(2)}) async-start(s8[8388608]{0:T(1024)(128)(4,1)} %bitcast.154), calls=%async_computation.2 | async-start | bytes 8388608
  33.2 9.6 %slice-start.1 = ((s8[8388608]{0:T(1024)(128)(4,1)}), s8[4194304]{0:T(1024)(128)(4,1)S(1)}, s32[]{:S(2)}) async-start(s8[8388608]{0:T(1024)(128)(4,1)} %bitcast.154), calls=%async_computation.3 | async-start | bytes 8388608
  52.6 10.9 %copy-start.4 = (f32[1,4,16,2048]{3,2,1,0:T(8,128)}, f32[1,4,16,2048]{3,2,1,0:T(8,128)S(1)}, u32[]{:S(2)}) copy-start(f32[1,4,16,2048]{3,2,1,0:T(8,128)S(1)} %collective-permute-done) | copy-start | bytes 1572868
  90.5 9.4 %copy-start = (f32[64,32,512]{2,1,0:T(8,128)S(1)}, f32[64,32,512]{2,1,0:T(8,128)}, u32[]{:S(2)}) copy-start(f32[64,32,512]{2,1,0:T(8,128)} %reshape_reshape.13) | copy-start | bytes 12582916
  108.9 8.8 %copy-start.1 = (f32[64,32,512]{2,1,0:T(8,128)S(1)}, f32[64,32,512]{2,1,0:T(8,128)}, u32[]{:S(2)}) copy-start(f32[64,32,512]{2,1,0:T(8,128)} %fusion.9) | copy-start | bytes 12582916
  117.6 4.0 %copy-start.2 = (f32[1,8,16,2048]{3,2,1,0:T(8,128)}, f32[1,8,16,2048]{3,2,1,0:T(8,128)S(1)}, u32[]{:S(2)}) copy-start(f32[1,8,16,2048]{3,2,1,0:T(8,128)S(1)} %collective-permute-done.1) | copy-start | bytes 3145732
  138.2 37.4 %collective-permute-start.2 = (f32[96,1024]{1,0:T(8,128)S(1)}, f32[96,1024]{1,0:T(8,128)S(1)}, u32[]{:S(2)}, u32[]{:S(2)}) collective-permute-start(f32[96,1024]{1,0:T(8,128)S(1)} %mul.1433), channel_id=1, source_target_pairs={{8,0},{10,2},{12,4},{14,6},{0,8},{2,10},{4,12},{6,14},{9,1},{11,3}... | collective-permute-start | bytes 1179656 | tf_op jit(solution)/shard_map/ppermute | solution.py:16
  140.6 53.2 %collective-permute-start.3 = (f32[96,1024]{1,0:T(8,128)S(1)}, f32[96,1024]{1,0:T(8,128)S(1)}, u32[]{:S(2)}, u32[]{:S(2)}) collective-permute-start(f32[96,1024]{1,0:T(8,128)S(1)} %mul.1433), channel_id=1, source_target_pairs={{10,0},{12,2},{14,4},{0,6},{2,8},{4,10},{6,12},{8,14},{11,1},{13,3... | collective-permute-start | bytes 1179656 | tf_op jit(solution)/shard_map/ppermute | solution.py:16
  143.1 50.8 %collective-permute-start.4 = (f32[96,1024]{1,0:T(8,128)S(1)}, f32[96,1024]{1,0:T(8,128)S(1)}, u32[]{:S(2)}, u32[]{:S(2)}) collective-permute-start(f32[96,1024]{1,0:T(8,128)S(1)} %mul.1433), channel_id=1, source_target_pairs={{12,0},{14,2},{0,4},{2,6},{4,8},{6,10},{8,12},{10,14},{13,1},{15,3... | collective-permute-start | bytes 1179656 | tf_op jit(solution)/shard_map/ppermute | solution.py:16
  143.1 51.1 %collective-permute-start.5 = (f32[96,1024]{1,0:T(8,128)S(1)}, f32[96,1024]{1,0:T(8,128)S(1)}, u32[]{:S(2)}, u32[]{:S(2)}) collective-permute-start(f32[96,1024]{1,0:T(8,128)S(1)} %mul.1433), channel_id=1, source_target_pairs={{14,0},{0,2},{2,4},{4,6},{6,8},{8,10},{10,12},{12,14},{15,1},{1,3}... | collective-permute-start | bytes 1179656 | tf_op jit(solution)/shard_map/ppermute | solution.py:16
  194.4 0.7 copy-start.11
  194.7 0.7 copy-start.10
  199.7 1.4 copy-start.9
  204.3 4.3 %copy-start.5 = (f32[1,4,16,2048]{3,2,1,0:T(8,128)S(1)}, f32[1,4,16,2048]{3,2,1,0:T(8,128)}, u32[]{:S(2)}) copy-start(f32[1,4,16,2048]{3,2,1,0:T(8,128)} %copy-done.4) | copy-start | bytes 1572868
  208.5 1.4 copy-start.3
  208.5 1.4 copy-start.6
  208.5 1.4 copy-start.7
  208.5 1.5 copy-start.8
  210.4 1.1 copy-start.12
where the time goes:
time: 217 us; the launch traced here: 212 us
  matrix products  64.5 us (30%)
  waiting for transfers between devices  48.7 us (22%)
  local copies, waits for them, and re-layouts  42.6 us (20%)
  other arithmetic  29.5 us (14%)
  blocking collectives  15 us (7%)
  starting transfers between devices  10 us (5%)
  between operations  2.2 us (1%)
    dot_general x14, matrix products, mixed(): jnp.einsum(form, left_op, right_op, precision=highest, preferred_element_...  64.5 us
    ppermute x6, waiting for transfers between devices, shifted(): return lax.ppermute(block, axis, route)  48.7 us
    all_to_all x1, blocking collectives, per_device(): lax.all_to_all(rows, 'sky', split_axis=1, concat_axis=0, tiled=True)  10.9 us
    ppermute x6, starting transfers between devices, shifted(): return lax.ppermute(block, axis, route)  10 us
    unnamed x38, local copies, waits for them, and re-layouts  8.15 us
    another operation x1, local copies, waits for them, and re-layouts, columns_forward(): spread_im.reshape(factor_one, second, col_count)  7.53 us
    another operation x1, local copies, waits for them, and re-layouts, columns_forward(): spread_re.reshape(factor_one, second, col_count)  7.51 us
    reduce_sum x1, other arithmetic, folded_spectra(): return jnp.transpose(jnp.sum(terms, axis=(1, 4)), (0, 2, 1, 3))  7.37 us
  transfers between devices with their start and end apart: 6, of which 3 were waited for; matrix products, arithmetic and copies ran while one was open for 47% of the time, Pallas kernels for 0%

commit v1 on v0

--- a/solution.py
+++ b/solution.py
@@ -204,7 +204,10 @@
     strength = lens_weight[0] * plane_count[0].astype(jnp.float32)
     rows = rows_forward(plane_cells)
     ray_first, rows = lax.optimization_barrier((ray_first, rows))
-    spread = lax.all_to_all(rows, "sky", split_axis=1, concat_axis=0, tiled=True)
+    spread = jnp.concatenate(
+        lax.all_to_all(jnp.stack(jnp.split(rows, lax.axis_size("sky"), axis=1)), "sky", 0, 0),
+        axis=0,
+    )
     k_local = spread.shape[1]
     spread_re = spread[:, :, :half].reshape(length, k_local * half)
     spread_im = spread[:, :, half:].reshape(length, k_local * half)

time: 217 us -> 218 us (level)
  transfers between devices with their start and end apart: 6 -> 6, of which waited for: 3 -> 3; matrix products, arithmetic and copies ran while one was open for 47% -> 48% of each run, Pallas kernels for 0% -> 0%
where the time goes in v1:
time: 218 us; the launch traced here: 214 us
  matrix products  64.5 us (30%)
  waiting for transfers between devices  48.8 us (22%)
  local copies, waits for them, and re-layouts  43.3 us (20%)
  other arithmetic  30 us (14%)
  blocking collectives  15 us (7%)
  starting transfers between devices  9.98 us (5%)
  between operations  2.21 us (1%)
    dot_general x14, matrix products, mixed(): jnp.einsum(form, left_op, right_op, precision=highest, preferred_element_...  64.5 us
    ppermute x6, waiting for transfers between devices, shifted(): return lax.ppermute(block, axis, route)  48.8 us
    all_to_all x1, blocking collectives, per_device(): lax.all_to_all(jnp.stack(jnp.split(rows, lax.axis_size('sky'), axis=1)),...  10.9 us
    ppermute x6, starting transfers between devices, shifted(): return lax.ppermute(block, axis, route)  9.98 us
    unnamed x38, local copies, waits for them, and re-layouts  8.19 us
    another operation x1, local copies, waits for them, and re-layouts, columns_forward(): spread_re.reshape(factor_one, second, col_count)  7.52 us
    another operation x1, local copies, waits for them, and re-layouts, columns_forward(): spread_im.reshape(factor_one, second, col_count)  7.51 us
    reduce_sum x1, other arithmetic, folded_spectra(): return jnp.transpose(jnp.sum(terms, axis=(1, 4)), (0, 2, 1, 3))  7.37 us
  transfers between devices with their start and end apart: 6, of which 3 were waited for; matrix products, arithmetic and copies ran while one was open for 48% of the time, Pallas kernels for 0%

profile of v1, /device:TPU:0, one launch (start us, length us, event | category | flops | bytes accessed | tf_op | source)
XLA Modules:
  0.0 213.7 jit_solution(11504497219756428325)
XLA Ops:
  0.0 1.9 slice.160
  1.9 4.0 %collective-permute-start = (f32[1,4,16,2048]{3,2,1,0:T(8,128)}, f32[1,4,16,2048]{3,2,1,0:T(8,128)S(1)}, u32[]{:S(2)}, u32[]{:S(2)}) collective-permute-start(f32[1,4,16,2048]{3,2,1,0:T(8,128)} %slice.160), channel_id=1, source_target_pairs={{8,0},{10,2},{12,4},{14,6},{0,8},{2,10},{4,12},{6,14},{9,1},{11,3}... | collective-permute-start | bytes 1572872 | tf_op jit(solution)/shard_map/ppermute | solution.py:16
  5.9 2.3 %slice.163 = f32[1,8,16,2048]{3,2,1,0:T(8,128)} slice(f32[1,12,16,2048]{3,2,1,0:T(8,128)} %param.7), slice={[0:1], [4:12], [0:16], [0:2048]} | slice | bytes 2097152 | tf_op jit(solution)/shard_map/slice | solution.py:197
  8.3 0.3 fusion.109
  8.6 0.3 fusion.113
  8.8 0.1 fusion.128
  9.0 0.1 fusion.127
  9.7 5.4 %copy.96 = f32[128,8,16,128]{3,2,1,0:T(8,128)S(1)} copy(f32[128,8,16,128]{3,1,2,0:T(8,128)} %bitcast.162) | data formatting | bytes 16777216
  15.0 6.0 %fusion.143 = f32[16,1024,128]{2,0,1:T(8,128)} fusion(f32[1024,16,128]{2,1,0:T(8,128)S(1)} %bitcast.150), kind=kOutput, calls=%fused_computation.242 | convolution fusion | flops 201330176 | bytes 16777216 | tf_op jit(solution)/shard_map/rvu,vk->rku/dot_general | solution.py:84
  22.4 10.8 %subtract_bitcast_fusion = (f32[1024,16,128]{2,1,0:T(8,128)}, f32[1024,16,128]{2,1,0:T(8,128)}) fusion(f32[16,1024,128]{2,0,1:T(8,128)} %fusion.143, f32[16,128]{1,0:T(8,128)S(1)} %get-tuple-element.91, f32[16,128]{1,0:T(8,128)S(1)} %get-tuple-element.92, f32[1024,16,128]{2,1,0:T(8,128)S(1)} %bitcast.151), kind=kOutput, calls=%fused_computation.10 | convolution fusion | flops 213913088 | bytes 33570816 | tf_op jit(solution)/shard_map/rvu,vk->rku/dot_general | solution.py:84
  33.2 9.6 %fusion.2 = f32[1024,16,128]{2,0,1:T(8,128)S(1)} fusion(f32[1024,16,128]{2,1,0:T(8,128)} %get-tuple-element.58, f32[128,64]{1,0:T(8,128)S(1)} %get-tuple-element.94, f32[128,64]{1,0:T(8,128)S(1)} %fusion.113), kind=kOutput, calls=%fused_computation.5 | convolution fusion | flops 1610629120 | bytes 16842752 | tf_op jit(solution)/shard_map/rkj,jn->rkn/dot_general | solution.py:84
  42.8 5.6 %fusion.15 = f32[1024,16,128]{2,0,1:T(8,128)S(1)} fusion(f32[1024,16,128]{2,0,1:T(8,128)S(1)} %fusion.2, f32[1024,16,128]{2,1,0:T(8,128)S(1)} %bitcast.156, f32[128,64]{1,0:T(8,128)S(1)} %get-tuple-element.93, f32[128,64]{1,0:T(8,128)S(1)} %get-tuple-element.94), kind=kOutput, calls=%fused_computation.29 | convolution fusion | flops 1612726272 | bytes 25231360 | tf_op jit(solution)/shard_map/rkj,jn->rkn/dot_general | solution.py:84
  48.4 3.6 %fusion.9 = f32[64,32,512]{2,1,0:T(8,128)} fusion(f32[512]{0:T(512)S(1)} %get-tuple-element.102, f32[64,32]{1,0:T(8,128)S(1)} %get-tuple-element.89, f32[512]{0:T(512)S(1)} %get-tuple-element.101, pred[512]{0:T(512)(128)(4,1)S(1)} %broadcast_compare_fusion, pred[64,32]{1,0:T(8,128)(4,1)S(1)} %fusion.108), kind=kLoop, calls=%fused_computation.16 | loop fusion | flops 9437184 | bytes 4209152 | tf_op jit(solution)/shard_map/mul | solution.py:185
  52.0 0.6 collective-permute-done
  52.6 0.8 slice_bitcast_fusion.1
  53.4 0.6 pad_maximum_fusion
  54.0 10.9 %all_to_all.14 = f32[2,1024,8,128]{3,1,2,0:T(8,128)S(1)} all-to-all(f32[2,1024,8,128]{3,1,2,0:T(8,128)S(1)} %pad_maximum_fusion), channel_id=1, replica_groups=mesh['real'=2,'los'=8,'sky'=2] {'sky'}, dimensions={0} | all-to-all | bytes 16777216 | tf_op jit(solution)/shard_map/all_to_all | solution.py:208
  64.9 4.9 %copy.76 = f32[2,1024,8,128]{3,2,1,0:T(8,128)S(1)} copy(f32[2,1024,8,128]{3,1,2,0:T(8,128)S(1)} %all_to_all.14) | data formatting | bytes 16777216 | tf_op jit(solution)/shard_map/all_to_all | solution.py:208
  69.8 7.1 %fusion.237 = (f32[2048,8,64]{2,1,0:T(8,128)}, f32[2048,8,64]{2,1,0:T(8,128)}) fusion(f32[2048,8,128]{2,1,0:T(8,128)S(1)} %bitcast.149), kind=kLoop, calls=%fused_computation.334 | loop fusion | bytes 16777216 | tf_op jit(solution)/shard_map/slice | solution.py:212
  76.9 7.5 %reshape_reshape.14 = f32[64,32,512]{2,1,0:T(8,128)} reshape(f32[2048,8,64]{2,1,0:T(8,128)} %get-tuple-element.62) | data formatting | bytes 8388608 | tf_op jit(solution)/shard_map/reshape;reshape | solution.py:133
  84.4 7.5 %reshape_reshape.13 = f32[64,32,512]{2,1,0:T(8,128)} reshape(f32[2048,8,64]{2,1,0:T(8,128)} %get-tuple-element.61) | data formatting | bytes 8388608 | tf_op jit(solution)/shard_map/reshape;reshape | solution.py:132
  91.9 9.4 %fusion.10 = f32[128,32,512]{2,0,1:T(8,128)S(1)} fusion(f32[64,32,512]{2,1,0:T(8,128)} %reshape_reshape.14, f32[64,64]{1,0:T(8,128)S(1)} %get-tuple-element.95, f32[64,64]{1,0:T(8,128)S(1)} %get-tuple-element.96), kind=kOutput, calls=%fused_computation.17 | convolution fusion | flops 805314560 | bytes 12615680 | tf_op jit(solution)/shard_map/jn,jbc->nbc/dot_general | solution.py:84
  101.4 5.9 %fusion.18 = f32[128,32,512]{2,0,1:T(8,128)S(1)} fusion(f32[128,32,512]{2,0,1:T(8,128)S(1)} %fusion.10, f32[64,32,512]{2,1,0:T(8,128)S(1)} %copy-done, f32[64,64]{1,0:T(8,128)S(1)} %fusion.127, f32[64,64]{1,0:T(8,128)S(1)} %get-tuple-element.95), kind=kOutput, calls=%fused_computation.30 | convolution fusion | flops 807411712 | bytes 21004288 | tf_op jit(solution)/shard_map/jn,jbc->nbc/dot_general | solution.py:84
  107.3 1.1 subtract_bitcast_fusion.1
  108.4 1.8 pad_maximum_fusion.1
  110.3 8.7 %fusion = f32[64,64,512]{2,0,1:T(8,128)S(1)} fusion(f32[64,64,512]{2,0,1:T(8,128)S(1)} %bitcast.153, f32[32,32]{0,1:T(8,128)S(1)} %get-tuple-element.100, f32[32,32]{0,1:T(8,128)S(1)} %fusion.164, f32[32,32]{0,1:T(8,128)S(1)} %get-tuple-element.99), kind=kOutput, calls=%fused_computation.3 | convolution fusion | flops 805318656 | bytes 16789504 | tf_op jit(solution)/shard_map/kjc,jn->knc/dot_general | solution.py:84
  119.0 4.0 %broadcast_multiply_fusion.1 = (f32[64,2,32,512]{3,2,1,0:T(8,128)}, f32[64,2,32,512]{3,2,1,0:T(8,128)S(1)}) fusion(f32[64,32]{1,0:T(8,128)S(1)} %get-tuple-element.90, f32[64,2,32,512]{3,2,1,0:T(8,128)S(1)} %bitcast.154, f32[64,32,512]{2,1,0:T(8,128)S(1)} %copy-done.1), kind=kLoop, calls=%fused_computation.22 | loop fusion | flops 4194304 | bytes 29368320 | tf_op jit(solution)/shard_map/mul | solution.py:187
  123.0 0.6 broadcast_multiply_fusion
  123.7 7.4 %maximum_reduce_fusion = f32[3,32,2,512]{3,2,1,0:T(2,128)S(1)} fusion(f32[1,2,32,2,32,512]{5,4,3,2,1,0:T(8,128)S(1)} %bitcast.152, f32[1,2,32,2,32,512]{5,4,3,2,1,0:T(8,128)} %bitcast.157, f32[1,2,32,2,32,512]{5,4,3,2,1,0:T(8,128)S(1)} %bitcast.148), kind=kLoop, calls=%fused_computation | loop fusion | flops 18776064 | bytes 25559040 | tf_op jit(solution)/shard_map/reduce_sum | solution.py:189
  131.1 0.4 convolution_bitcast_fusion
  131.5 0.2 reshape.933
  131.7 0.5 reshape.946
  132.2 4.0 %all_to_all.15 = f32[2,1,49152]{2,1,0:T(1,128)S(1)} all-to-all(f32[2,1,49152]{2,1,0:T(1,128)S(1)} %reshape.946), channel_id=1, replica_groups=mesh['real'=2,'los'=8,'sky'=2] {'sky'}, dimensions={0} | all-to-all | bytes 786432 | tf_op jit(solution)/shard_map/all_to_all | solution.py:223
  136.3 0.5 broadcast.706
  136.7 1.8 reduce
  138.5 0.5 reshape.947
  139.1 0.2 mul.1433
  139.4 2.4 %collective-permute-start.2 = (f32[96,1024]{1,0:T(8,128)S(1)}, f32[96,1024]{1,0:T(8,128)S(1)}, u32[]{:S(2)}, u32[]{:S(2)}) collective-permute-start(f32[96,1024]{1,0:T(8,128)S(1)} %mul.1433), channel_id=1, source_target_pairs={{8,0},{10,2},{12,4},{14,6},{0,8},{2,10},{4,12},{6,14},{9,1},{11,3}... | collective-permute-start | bytes 1179656 | tf_op jit(solution)/shard_map/ppermute | solution.py:16
  141.8 2.5 %collective-permute-start.3 = (f32[96,1024]{1,0:T(8,128)S(1)}, f32[96,1024]{1,0:T(8,128)S(1)}, u32[]{:S(2)}, u32[]{:S(2)}) collective-permute-start(f32[96,1024]{1,0:T(8,128)S(1)} %mul.1433), channel_id=1, source_target_pairs={{10,0},{12,2},{14,4},{0,6},{2,8},{4,10},{6,12},{8,14},{11,1},{13,3... | collective-permute-start | bytes 1179656 | tf_op jit(solution)/shard_map/ppermute | solution.py:16
  144.3 1.0 collective-permute-start.5
  145.3 0.7 multiply_sine_fusion.2
  146.0 0.6 fusion.140
  146.6 30.2 %collective-permute-done.2 = f32[96,1024]{1,0:T(8,128)S(1)} collective-permute-done((f32[96,1024]{1,0:T(8,128)S(1)}, f32[96,1024]{1,0:T(8,128)S(1)}, u32[]{:S(2)}, u32[]{:S(2)}) %collective-permute-start.2) | collective-permute-done | bytes 393248 | tf_op jit(solution)/shard_map/ppermute | solution.py:16
  176.8 0.2 stack.85
  177.0 17.9 %collective-permute-done.3 = f32[96,1024]{1,0:T(8,128)S(1)} collective-permute-done((f32[96,1024]{1,0:T(8,128)S(1)}, f32[96,1024]{1,0:T(8,128)S(1)}, u32[]{:S(2)}, u32[]{:S(2)}) %collective-permute-start.3) | collective-permute-done | bytes 393248 | tf_op jit(solution)/shard_map/ppermute | solution.py:16
  194.9 0.2 stack.86
  195.2 0.2 stack.87
  195.4 0.2 stack.88
  195.6 0.3 pad_maximum_fusion.2
  195.9 0.4 copy-done.11
  196.5 0.2 copy-done.10
  196.9 1.3 fusion.102
  198.2 1.3 fusion.98
  199.5 1.3 convolution_subtract_fusion
  200.9 1.4 convolution_add_fusion
  202.3 1.3 fusion.21
  203.6 1.3 subtract_bitcast_fusion.2
  205.0 0.2 fusion.238
  205.5 2.2 %add_subtract_fusion.6 = (f32[1,1,16,2048]{3,2,1,0:T(8,128)S(1)}, f32[1,1,16,2048]{3,2,1,0:T(8,128)S(1)}, f32[1,1,16,2048]{3,2,1,0:T(8,128)S(1)}, f32[1,1,16,204...) fusion(f32[1,5,16,2048]{3,2,1,0:T(8,128)S(1)} %slice.181, f32[1,8,16,2048]{3,2,1,0:T(8,128)} %copy-done.2, ...), kind=kLoop, calls=%fused_computation.102 | loop fusion | flops 917504 | bytes 2490368 | tf_op jit(solution)/shard_map/sub | solution.py:44
  207.7 1.9 fusion.55
  209.8 1.2 fusion.51
  211.2 0.1 add_subtract_fusion.4
  211.6 1.1 copy-done.12
  212.8 0.7 constant_dynamic-update-slice_fusion
  (69 shorter events, 2.1 us)
Async XLA Ops:
  1.9 50.7 %collective-permute-start = (f32[1,4,16,2048]{3,2,1,0:T(8,128)}, f32[1,4,16,2048]{3,2,1,0:T(8,128)S(1)}, u32[]{:S(2)}, u32[]{:S(2)}) collective-permute-start(f32[1,4,16,2048]{3,2,1,0:T(8,128)} %slice.160), channel_id=1, source_target_pairs={{8,0},{10,2},{12,4},{14,6},{0,8},{2,10},{4,12},{6,14},{9,1},{11,3}... | collective-permute-start | bytes 1572872 | tf_op jit(solution)/shard_map/ppermute | solution.py:16
  8.2 110.8 %collective-permute-start.1 = (f32[1,8,16,2048]{3,2,1,0:T(8,128)}, f32[1,8,16,2048]{3,2,1,0:T(8,128)S(1)}, u32[]{:S(2)}, u32[]{:S(2)}) collective-permute-start(f32[1,8,16,2048]{3,2,1,0:T(8,128)} %slice.163), channel_id=1, source_target_pairs={{8,0},{10,2},{12,4},{14,6},{0,8},{2,10},{4,12},{6,14},{9,1},{11,3}... | collective-permute-start | bytes 3145736 | tf_op jit(solution)/shard_map/ppermute | solution.py:16
  33.2 9.6 %slice-start = ((s8[8388608]{0:T(1024)(128)(4,1)}), s8[4194304]{0:T(1024)(128)(4,1)S(1)}, s32[]{:S(2)}) async-start(s8[8388608]{0:T(1024)(128)(4,1)} %bitcast.155), calls=%async_computation.2 | async-start | bytes 8388608
  33.2 9.6 %slice-start.1 = ((s8[8388608]{0:T(1024)(128)(4,1)}), s8[4194304]{0:T(1024)(128)(4,1)S(1)}, s32[]{:S(2)}) async-start(s8[8388608]{0:T(1024)(128)(4,1)} %bitcast.155), calls=%async_computation.3 | async-start | bytes 8388608
  52.6 0.8 copy-start.4
  91.9 9.4 %copy-start = (f32[64,32,512]{2,1,0:T(8,128)S(1)}, f32[64,32,512]{2,1,0:T(8,128)}, u32[]{:S(2)}) copy-start(f32[64,32,512]{2,1,0:T(8,128)} %reshape_reshape.13) | copy-start | bytes 12582916
  110.2 8.8 %copy-start.1 = (f32[64,32,512]{2,1,0:T(8,128)S(1)}, f32[64,32,512]{2,1,0:T(8,128)}, u32[]{:S(2)}) copy-start(f32[64,32,512]{2,1,0:T(8,128)} %fusion.9) | copy-start | bytes 12582916
  119.0 4.0 %copy-start.2 = (f32[1,8,16,2048]{3,2,1,0:T(8,128)}, f32[1,8,16,2048]{3,2,1,0:T(8,128)S(1)}, u32[]{:S(2)}) copy-start(f32[1,8,16,2048]{3,2,1,0:T(8,128)S(1)} %collective-permute-done.1) | copy-start | bytes 3145732
  139.4 37.4 %collective-permute-start.2 = (f32[96,1024]{1,0:T(8,128)S(1)}, f32[96,1024]{1,0:T(8,128)S(1)}, u32[]{:S(2)}, u32[]{:S(2)}) collective-permute-start(f32[96,1024]{1,0:T(8,128)S(1)} %mul.1433), channel_id=1, source_target_pairs={{8,0},{10,2},{12,4},{14,6},{0,8},{2,10},{4,12},{6,14},{9,1},{11,3}... | collective-permute-start | bytes 1179656 | tf_op jit(solution)/shard_map/ppermute | solution.py:16
  141.8 53.2 %collective-permute-start.3 = (f32[96,1024]{1,0:T(8,128)S(1)}, f32[96,1024]{1,0:T(8,128)S(1)}, u32[]{:S(2)}, u32[]{:S(2)}) collective-permute-start(f32[96,1024]{1,0:T(8,128)S(1)} %mul.1433), channel_id=1, source_target_pairs={{10,0},{12,2},{14,4},{0,6},{2,8},{4,10},{6,12},{8,14},{11,1},{13,3... | collective-permute-start | bytes 1179656 | tf_op jit(solution)/shard_map/ppermute | solution.py:16
  144.3 50.9 %collective-permute-start.4 = (f32[96,1024]{1,0:T(8,128)S(1)}, f32[96,1024]{1,0:T(8,128)S(1)}, u32[]{:S(2)}, u32[]{:S(2)}) collective-permute-start(f32[96,1024]{1,0:T(8,128)S(1)} %mul.1433), channel_id=1, source_target_pairs={{12,0},{14,2},{0,4},{2,6},{4,8},{6,10},{8,12},{10,14},{13,1},{15,3... | collective-permute-start | bytes 1179656 | tf_op jit(solution)/shard_map/ppermute | solution.py:16
  144.3 51.1 %collective-permute-start.5 = (f32[96,1024]{1,0:T(8,128)S(1)}, f32[96,1024]{1,0:T(8,128)S(1)}, u32[]{:S(2)}, u32[]{:S(2)}) collective-permute-start(f32[96,1024]{1,0:T(8,128)S(1)} %mul.1433), channel_id=1, source_target_pairs={{14,0},{0,2},{2,4},{4,6},{6,8},{8,10},{10,12},{12,14},{15,1},{1,3}... | collective-permute-start | bytes 1179656 | tf_op jit(solution)/shard_map/ppermute | solution.py:16
  195.6 0.7 copy-start.11
  195.9 0.7 copy-start.10
  200.9 1.4 copy-start.9
  205.5 4.3 %copy-start.5 = (f32[1,4,16,2048]{3,2,1,0:T(8,128)S(1)}, f32[1,4,16,2048]{3,2,1,0:T(8,128)}, u32[]{:S(2)}) copy-start(f32[1,4,16,2048]{3,2,1,0:T(8,128)} %copy-done.4) | copy-start | bytes 1572868
  209.7 1.4 copy-start.3
  209.7 1.4 copy-start.6
  209.7 1.4 copy-start.7
  209.7 1.5 copy-start.8
  211.6 1.1 copy-start.12
